TPU v7x, 256 devices: a whole 4x4x8 slice. The times are simulated.
256 devices in a mesh: row: 16 (over z, x_lo), col: 4 (over x_hi, core), layer: 4 (over y).
Axes of the slice: x: 4 (x_hi: 2, x_lo: 2; x = x_hi * 2 + x_lo), y: 4, z: 8, core: 2. Of those that a mesh axis runs over, the one named last changes fastest.
Arguments:
- density: bfloat16 [512, 16, 128, 128], P('row', 'col'), may hold values from -0.59765625 to 0.59765625
- block_offset: int32 [512, 16], P('row', 'col'), may hold values from 0 to 1, as said below
- filter_offset: int32 [64, 32], P('row', 'col'), may hold values from 0 to 3, as said below
- position: int32 [32], replicated, may hold values from 0 to 31, each once
Outputs:
- purified: float32 [64, 32, 128, 128], P(('row', 'layer'), 'col')
Inputs may be any that keep to these rules, and one draw needn't show every extreme that they name: `block_offset`: slots fall into groups of 1 consecutive slots; within each group of a block row the offsets rise strictly (a group of one slot holds a single offset). `filter_offset`: slots fall into groups of 2 consecutive slots; within each group of a row the offsets rise strictly (a group of one slot holds a single offset).
All inputs are finite; a program needn't handle non-finite values.
Results may differ from a plain program's by a relative error of at most 0.0027.
Values may be sent and summed in bfloat16 or wider, within the bound.
No kernel may reach another device: no remote copies, remote signals or barrier semaphores. Data moves between devices by JAX's collectives and lax.ppermute only.
A program may use at most 128 MiB of HBM per device.

v0:
```python
import jax
import jax.numpy as jnp
from jax import lax
from jax.sharding import PartitionSpec as P

W = 16
WF = 32
RA = 4


def from_behind(value, axis, steps):
    count = lax.axis_size(axis)
    pairs = [(source, (source + steps) % count) for source in range(count)]
    return lax.ppermute(value, axis, pairs)


def column_index(offsets, local_rows, position, image_of, slot_base, group_size):
    extent = position.shape[0]
    groups = (slot_base + jnp.arange(offsets.shape[1], dtype=jnp.int32)) // group_size * extent
    physical = (position[local_rows][:, None] + offsets) % extent
    return groups[None, :] + image_of[physical]


def block_multiply(left_blocks, local_rows, right_blocks, right_columns, targets):
    picked = right_blocks[local_rows]
    picked_columns = right_columns[local_rows]
    matches = picked_columns[:, :, None, :] == targets[:, None, :, None]
    chosen = jnp.einsum(
        "nsut,nstyz->nsuyz",
        matches.astype(jnp.bfloat16),
        picked,
        preferred_element_type=jnp.float32,
    ).astype(jnp.bfloat16)
    return jnp.einsum("nsxy,nsuyz->nuxz", left_blocks, chosen, preferred_element_type=jnp.float32)


def on_device(density, block_offset, filter_offset, position):
    rows_tile = density.shape[0]
    slots_tile = density.shape[1]
    edge = density.shape[2]
    row_count = lax.axis_size("row")
    layer_count = lax.axis_size("layer")
    group_block = W // row_count
    group_filter = WF // row_count
    filter_slots = filter_offset.shape[1]
    row_id = lax.axis_index("row")
    col_id = lax.axis_index("col")
    layer_id = lax.axis_index("layer")
    extent = position.shape[0]
    image_of = jnp.zeros((extent,), jnp.int32).at[position].set(jnp.arange(extent, dtype=jnp.int32))
    right_columns = column_index(
        block_offset,
        jnp.arange(rows_tile, dtype=jnp.int32),
        position,
        image_of,
        col_id * slots_tile,
        group_block,
    )
    target_columns = column_index(
        filter_offset,
        jnp.arange(RA, dtype=jnp.int32),
        position,
        image_of,
        col_id * filter_slots,
        group_filter,
    )
    share_rows = RA // layer_count
    step_count = row_count // layer_count
    carried = (density, right_columns)
    for bit_number in range(layer_count.bit_length() - 1):
        moved = from_behind((carried[0], carried[1]), "row", step_count * (1 << bit_number))
        taken = layer_id >> bit_number & 1 == 1
        carried = (jnp.where(taken, moved[0], carried[0]), jnp.where(taken, moved[1], carried[1]))
    panels = []
    for turn_index in range(step_count):
        if turn_index > 0:
            carried = from_behind((carried[0], carried[1]), "row", 1)
        source = (row_id - layer_id * step_count - turn_index) % row_count
        panels.append((source, carried))

    def gather_left(left_blocks, left_columns):
        return (
            lax.all_gather(left_blocks, "col", axis=1, tiled=True),
            lax.all_gather(left_columns, "col", axis=1, tiled=True),
        )

    def panel_product(left_blocks, left_columns, group_size):
        full_blocks, full_columns = gather_left(left_blocks, left_columns)
        running = jnp.zeros((RA, filter_slots, edge, edge), jnp.float32)
        for source, received in panels:
            start = source * group_size
            piece = lax.dynamic_slice_in_dim(full_blocks, start, group_size, 1)
            piece_columns = lax.dynamic_slice_in_dim(full_columns, start, group_size, 1)
            running = running + block_multiply(
                piece, piece_columns - source * rows_tile, received[0], received[1], target_columns
            )
        return running

    square = panel_product(density[:RA], right_columns[:RA], group_block)
    summed = lax.psum(square, "layer")
    square_own = lax.dynamic_slice_in_dim(summed, layer_id * share_rows, share_rows, 0)
    square_half = summed.astype(jnp.bfloat16)
    cube = panel_product(square_half, target_columns, group_filter)
    cube_own = lax.psum_scatter(cube, "layer", scatter_dimension=0, tiled=True)
    return 3.0 * square_own - 2.0 * cube_own


def solution(mesh):
    placed = (P("row", "col", None, None), P("row", "col"), P("row", "col"), P())
    return jax.shard_map(
        on_device,
        mesh=mesh,
        in_specs=placed,
        out_specs=P(("row", "layer"), "col", None, None),
        check_vma=False,
    )
```

profile of v0, /device:TPU:1, one launch (start us, length us, event | category | flops | bytes accessed | tf_op | source)
XLA Modules:
  0.0 888.2 jit_solution(15324507685565275466)
XLA Ops:
  6.5 3.8 collective-permute-start.2
  10.3 130.0 %collective-permute-done.2 = bf16[32,4,128,128]{3,2,1,0:T(8,128)(2,1)} collective-permute-done((bf16[32,4,128,128]{3,2,1,0:T(8,128)(2,1)}, bf16[32,4,128,128]{3,2,1,0:T(8,128)(2,1)}, u32[]{:S(2)}, u32[]{:S(2)}) %collective-permute-start.2) | collective-permute-done | bytes 4194336 | tf_op jit(solution)/shard_map/ppermute | solution.py:14
  140.3 4.6 broadcast_select_fusion
  144.9 58.2 %collective-permute-start.3 = (bf16[32,4,128,128]{3,2,1,0:T(8,128)(2,1)}, bf16[32,4,128,128]{3,2,1,0:T(8,128)(2,1)}, u32[]{:S(2)}, u32[]{:S(2)}) collective-permute-start(bf16[32,4,128,128]{3,2,1,0:T(8,128)(2,1)} %broadcast_select_fusion), channel_id=1, source_target_pairs={{0,128},{16,144},{32,160},{48,176},{64,192},{80,208},{96,224},{112... | collective-permute-start | bytes 12582920 | tf_op jit(solution)/shard_map/ppermute | solution.py:14
  203.1 180.2 %collective-permute-done.3 = bf16[32,4,128,128]{3,2,1,0:T(8,128)(2,1)} collective-permute-done((bf16[32,4,128,128]{3,2,1,0:T(8,128)(2,1)}, bf16[32,4,128,128]{3,2,1,0:T(8,128)(2,1)}, u32[]{:S(2)}, u32[]{:S(2)}) %collective-permute-start.3) | collective-permute-done | bytes 4194336 | tf_op jit(solution)/shard_map/ppermute | solution.py:14
  383.3 2.6 broadcast_select_fusion.1
  385.9 1.9 copy-done.3
  387.9 1.2 collective-permute-start.5
  389.1 92.5 %collective-permute-done.5 = bf16[32,4,128,128]{3,2,1,0:T(8,128)(2,1)} collective-permute-done((bf16[32,4,128,128]{3,2,1,0:T(8,128)(2,1)S(1)}, bf16[32,4,128,128]{3,2,1,0:T(8,128)(2,1)}, u32[]{:S(2)}, u32[]{:S(2)}) %collective-permute-start.5) | collective-permute-done | bytes 4194336 | tf_op jit(solution)/shard_map/ppermute | solution.py:14
  481.6 0.4 collective-permute-start.7
  482.0 0.7 gather_fusion
  483.0 0.7 scatter_custom_fusion
  483.7 1.2 gather_fusion.1
  485.0 2.1 collective-permute-start
  487.2 1.9 slice.7
  489.2 0.6 gather_fusion.3
  490.0 92.1 %collective-permute-done.7 = bf16[32,4,128,128]{3,2,1,0:T(8,128)(2,1)} collective-permute-done((bf16[32,4,128,128]{3,2,1,0:T(8,128)(2,1)}, bf16[32,4,128,128]{3,2,1,0:T(8,128)(2,1)}, u32[]{:S(2)}, u32[]{:S(2)}) %collective-permute-start.7) | collective-permute-done | bytes 4194336 | tf_op jit(solution)/shard_map/ppermute | solution.py:14
  582.1 2.2 collective-permute-start.9
  584.3 0.7 gather_fusion.4
  585.2 94.4 %all-gather = s32[4,4,4]{2,1,0:T(4,128)S(1)} all-gather(s32[1,4,4]{2,1,0:T(4,128)S(1)} %bitcast.166), channel_id=1, replica_groups=mesh['row'=16,'col'=4,'layer'=4] {'col'}, dimensions={0}, use_global_device_ids=true | all-gather | bytes 320 | tf_op jit(solution)/shard_map/all_gather | solution.py:84
  680.4 5.3 collective-permute-start.1
  685.7 1.4 collective-permute-done.1
  687.1 4.7 collective-permute-done.4
  691.8 4.7 collective-permute-done.6
  696.5 0.6 gather_fusion.2
  697.1 0.6 gather_fusion.6
  697.6 0.6 gather_fusion.8
  698.2 3.0 collective-permute-done.8
  701.2 0.6 gather_fusion.10
  701.8 2.8 gather_fusion.5
  704.6 0.6 convolution_convert_fusion.7
  705.3 1.4 fusion.20
  706.7 2.8 gather_fusion.7
  709.6 0.6 convolution_convert_fusion.6
  710.2 2.8 fusion.18
  713.0 2.8 gather_fusion.9
  715.8 0.6 convolution_convert_fusion.5
  716.5 2.8 fusion.16
  719.2 2.8 gather_fusion.11
  722.1 0.6 convolution_convert_fusion.4
  722.7 4.2 add_bitcast_fusion
  727.0 66.7 %all-reduce.2.cloned.1.call-done = f32[4,8,128,128]{2,3,1,0:T(8,128)} async-done(((f32[4,8,128,128]{2,3,1,0:T(8,128)}), f32[4,8,128,128]{2,3,1,0:T(8,128)}) %all-reduce.2.cloned.1.call-update) | async-done | bytes 2097168 | tf_op jit(solution)/shard_map/psum | solution.py:100
  793.7 2.7 convert_element_type.44
  796.6 7.6 all-gather.1
  804.7 0.6 gather_fusion.12
  805.3 0.6 gather_fusion.14
  805.8 0.6 gather_fusion.16
  806.4 0.6 gather_fusion.18
  806.9 3.3 gather_fusion.13
  810.3 2.2 convolution_convert_fusion.3
  812.5 2.9 gather_fusion.15
  815.4 1.2 convolution_convert_fusion.2
  816.7 3.0 gather_fusion.17
  819.6 2.2 convolution_convert_fusion.1
  821.9 3.0 gather_fusion.19
  824.9 2.2 convolution_convert_fusion
  827.1 10.9 %all-gather.7.cloned.1.call-done = bf16[4,32,128,128]{2,3,1,0:T(8,128)(2,1)} async-done(((bf16[4,8,128,128]{2,3,1,0:T(8,128)(2,1)}), bf16[4,32,128,128]{2,3,1,0:T(8,128)(2,1)}) %all-gather.7.cloned.1.call-update) | async-done | bytes 4194320 | tf_op jit(solution)/shard_map/all_gather | solution.py:83
  838.0 2.7 fusion.1
  840.7 1.9 fusion.3
  842.6 2.0 fusion.5
  844.6 3.3 fusion
  848.0 31.4 %reduce-scatter.2.cloned.1.call-done = f32[1,8,128,128]{2,3,1,0:T(8,128)} async-done(((f32[4,8,128,128]{2,3,1,0:T(8,128)}), f32[1,8,128,128]{2,3,1,0:T(8,128)}) %reduce-scatter.2.cloned.1.call-update) | async-done | bytes 524304 | tf_op jit(solution)/shard_map/reduce_scatter | solution.py:104
  879.4 1.3 multiply_subtract_fusion
  880.7 1.0 copy.47
  (75 shorter events, 2.2 us)
Async XLA Ops:
  6.5 698.7 %all-gather.5.cloned.1.call-start = ((), (), s32[]{:S(2)}) async-start(), calls=%async_computation.1 | async-start | bytes 2621440 | tf_op jit(solution)/shard_map/all_gather | solution.py:83
  6.5 133.8 %collective-permute-start.2 = (bf16[32,4,128,128]{3,2,1,0:T(8,128)(2,1)}, bf16[32,4,128,128]{3,2,1,0:T(8,128)(2,1)}, u32[]{:S(2)}, u32[]{:S(2)}) collective-permute-start(bf16[32,4,128,128]{3,2,1,0:T(8,128)(2,1)} %param.4), channel_id=1, source_target_pairs={{0,64},{16,80},{32,96},{48,112},{64,128},{80,144},{96,160},{112,17... | collective-permute-start | bytes 12582920 | tf_op jit(solution)/shard_map/ppermute | solution.py:14
  144.9 238.4 %collective-permute-start.3 = (bf16[32,4,128,128]{3,2,1,0:T(8,128)(2,1)}, bf16[32,4,128,128]{3,2,1,0:T(8,128)(2,1)}, u32[]{:S(2)}, u32[]{:S(2)}) collective-permute-start(bf16[32,4,128,128]{3,2,1,0:T(8,128)(2,1)} %broadcast_select_fusion), channel_id=1, source_target_pairs={{0,128},{16,144},{32,160},{48,176},{64,192},{80,208},{96,224},{112... | collective-permute-start | bytes 12582920 | tf_op jit(solution)/shard_map/ppermute | solution.py:14
  203.1 278.9 %copy-start = (s32[32]{0:T(128)S(1)}, s32[32]{0:T(128)}, u32[]{:S(2)}) copy-start(s32[32]{0:T(128)} %param.7) | copy-start | bytes 388
  203.1 279.6 %copy-start.4 = (s32[32,4]{0,1:T(4,128)S(1)}, s32[32,4]{0,1:T(4,128)}, u32[]{:S(2)}) copy-start(s32[32,4]{0,1:T(4,128)} %param.5) | copy-start | bytes 1540
  385.9 2.0 copy-start.3
  387.9 93.8 %collective-permute-start.5 = (bf16[32,4,128,128]{3,2,1,0:T(8,128)(2,1)S(1)}, bf16[32,4,128,128]{3,2,1,0:T(8,128)(2,1)}, u32[]{:S(2)}, u32[]{:S(2)}) collective-permute-start(bf16[32,4,128,128]{3,2,1,0:T(8,128)(2,1)S(1)} %broadcast_select_fusion.1), channel_id=1, source_target_pairs={{0,16},{16,32},{32,48},{48,64},{64,80},{80,96},{96,112},{112,128},... | collective-permute-start | bytes 12582920 | tf_op jit(solution)/shard_map/ppermute | solution.py:14
  481.6 100.5 %collective-permute-start.7 = (bf16[32,4,128,128]{3,2,1,0:T(8,128)(2,1)}, bf16[32,4,128,128]{3,2,1,0:T(8,128)(2,1)}, u32[]{:S(2)}, u32[]{:S(2)}) collective-permute-start(bf16[32,4,128,128]{3,2,1,0:T(8,128)(2,1)} %collective-permute-done.5), channel_id=1, source_target_pairs={{0,16},{16,32},{32,48},{48,64},{64,80},{80,96},{96,112},{112,128},... | collective-permute-start | bytes 12582920 | tf_op jit(solution)/shard_map/ppermute | solution.py:14
  484.9 4.9 copy-start.5
  485.0 195.3 %collective-permute-start = (s32[32,4]{1,0:T(8,128)S(1)}, s32[32,4]{1,0:T(8,128)S(1)}, u32[]{:S(2)}, u32[]{:S(2)}) collective-permute-start(s32[32,4]{1,0:T(8,128)S(1)} %broadcast_add_fusion), channel_id=1, source_target_pairs={{0,64},{16,80},{32,96},{48,112},{64,128},{80,144},{96,160},{112,17... | collective-permute-start | bytes 1544 | tf_op jit(solution)/shard_map/ppermute | solution.py:14
  489.1 304.6 %all-reduce.2.cloned.1.call-start = ((), (), s32[]{:S(2)}) async-start(), calls=%async_computation.2 | async-start | bytes 4194304 | tf_op jit(solution)/shard_map/psum | solution.py:100
  582.1 137.1 %collective-permute-start.9 = (bf16[32,4,128,128]{3,2,1,0:T(8,128)(2,1)}, bf16[32,4,128,128]{3,2,1,0:T(8,128)(2,1)}, u32[]{:S(2)}, u32[]{:S(2)}) collective-permute-start(bf16[32,4,128,128]{3,2,1,0:T(8,128)(2,1)} %collective-permute-done.7), channel_id=1, source_target_pairs={{0,16},{16,32},{32,48},{48,64},{64,80},{80,96},{96,112},{112,128},... | collective-permute-start | bytes 12582920 | tf_op jit(solution)/shard_map/ppermute | solution.py:14
  680.4 6.7 collective-permute-start.1
  687.1 4.7 collective-permute-start.4
  691.8 4.7 collective-permute-start.6
  696.5 4.7 collective-permute-start.8
  727.0 111.1 %all-gather.7.cloned.1.call-start = ((), (), s32[]{:S(2)}) async-start(), calls=%async_computation.3 | async-start | bytes 5242880 | tf_op jit(solution)/shard_map/all_gather | solution.py:83
  796.5 82.9 %reduce-scatter.2.cloned.1.call-start = ((), (), s32[]{:S(2)}) async-start(), calls=%async_computation.4 | async-start | bytes 2621440 | tf_op jit(solution)/shard_map/reduce_scatter | solution.py:104
  838.0 2.7 copy-start.1
  842.6 2.0 copy-start.2
Sparse Core Ops, SparseCore 0:
  489.2 41.7 all-gather.4
  727.1 66.5 all-reduce.1
  796.6 41.3 all-gather.6
  848.1 31.2 reduce-scatter.1
where the time goes:
time: 889 us; the launch traced here: 888 us
  waiting for transfers between devices  618 us (70%)
  blocking collectives  102 us (11%)
  starting transfers between devices  73.4 us (8%)
  local copies, waits for them, and re-layouts  38.1 us (4%)
  matrix products  31.5 us (4%)
  between operations  13.6 us (2%)
  other arithmetic  11.8 us (1%)
    ppermute x10, waiting for transfers between devices, from_behind(): return lax.ppermute(value, axis, pairs)  509 us
    all_gather x2, blocking collectives, gather_left(): lax.all_gather(left_columns, 'col', axis=1, tiled=True)  102 us
    ppermute x10, starting transfers between devices, from_behind(): return lax.ppermute(value, axis, pairs)  73.2 us
    psum x1, waiting for transfers between devices, on_device(): summed = lax.psum(square, 'layer')  66.7 us
    reduce_scatter x1, waiting for transfers between devices, on_device(): cube_own = lax.psum_scatter(cube, 'layer', scatter_dimension=0, tiled=True)  31.4 us
    gather x8, local copies, waits for them, and re-layouts, block_multiply(): picked = right_blocks[local_rows]  23.5 us
    dot_general x8, matrix products, block_multiply(): jnp.einsum('nsxy,nsuyz->nuxz', left_blocks, chosen, preferred_element_typ...  21.1 us
  transfers between devices with their start and end apart: 14, of which 11 were waited for; matrix products, arithmetic and copies ran while one was open for 6% of the time, Pallas kernels for 0%

commit v1 on v0

--- a/solution.py
+++ b/solution.py
@@ -97,7 +97,7 @@
         return running
 
     square = panel_product(density[:RA], right_columns[:RA], group_block)
-    summed = lax.psum(square, "layer")
+    summed = jnp.sum(lax.all_gather(square, "layer"), axis=0)
     square_own = lax.dynamic_slice_in_dim(summed, layer_id * share_rows, share_rows, 0)
     square_half = summed.astype(jnp.bfloat16)
     cube = panel_product(square_half, target_columns, group_filter)

time: 889 us -> 918 us (1.033)
  waiting for transfers between devices: 618 us -> 640 us
    all_gather x0 -> x1, waiting for transfers between devices: none -> 88.5 us  [on_device(): summed = jnp.sum(lax.all_gather(square, 'layer'), axis=0)]
    psum x1 -> x0, waiting for transfers between devices: 66.7 us -> none  [on_device(): summed = lax.psum(square, 'layer')]
where the time goes in v1:
time: 918 us; the launch traced here: 917 us
  waiting for transfers between devices  640 us (70%)
  blocking collectives  102 us (11%)
  starting transfers between devices  73.4 us (8%)
  local copies, waits for them, and re-layouts  41.1 us (4%)
  matrix products  32.7 us (4%)
  other arithmetic  14.6 us (2%)
  between operations  13.6 us (1%)
    ppermute x10, waiting for transfers between devices, from_behind(): return lax.ppermute(value, axis, pairs)  509 us
    all_gather x2, blocking collectives, gather_left(): lax.all_gather(left_columns, 'col', axis=1, tiled=True)  102 us
    all_gather x1, waiting for transfers between devices, on_device(): summed = jnp.sum(lax.all_gather(square, 'layer'), axis=0)  88.5 us
    ppermute x10, starting transfers between devices, from_behind(): return lax.ppermute(value, axis, pairs)  73.2 us
    reduce_scatter x1, waiting for transfers between devices, on_device(): cube_own = lax.psum_scatter(cube, 'layer', scatter_dimension=0, tiled=True)  31.2 us
    gather x8, local copies, waits for them, and re-layouts, block_multiply(): picked = right_blocks[local_rows]  23.4 us
    dot_general x8, matrix products, block_multiply(): jnp.einsum('nsxy,nsuyz->nuxz', left_blocks, chosen, preferred_element_typ...  21.2 us
  transfers between devices with their start and end apart: 14, of which 11 were waited for; matrix products, arithmetic and copies ran while one was open for 6% of the time, Pallas kernels for 0%

profile of v1, /device:TPU:1, one launch (start us, length us, event | category | flops | bytes accessed | tf_op | source)
XLA Modules:
  0.0 917.1 jit_solution(1635960470194171062)
XLA Ops:
  6.5 3.8 collective-permute-start.2
  10.3 130.0 %collective-permute-done.2 = bf16[32,4,128,128]{3,2,1,0:T(8,128)(2,1)} collective-permute-done((bf16[32,4,128,128]{3,2,1,0:T(8,128)(2,1)}, bf16[32,4,128,128]{3,2,1,0:T(8,128)(2,1)}, u32[]{:S(2)}, u32[]{:S(2)}) %collective-permute-start.2) | collective-permute-done | bytes 4194336 | tf_op jit(solution)/shard_map/ppermute | solution.py:14
  140.3 4.6 broadcast_select_fusion
  144.9 58.2 %collective-permute-start.3 = (bf16[32,4,128,128]{3,2,1,0:T(8,128)(2,1)}, bf16[32,4,128,128]{3,2,1,0:T(8,128)(2,1)}, u32[]{:S(2)}, u32[]{:S(2)}) collective-permute-start(bf16[32,4,128,128]{3,2,1,0:T(8,128)(2,1)} %broadcast_select_fusion), channel_id=1, source_target_pairs={{0,128},{16,144},{32,160},{48,176},{64,192},{80,208},{96,224},{112... | collective-permute-start | bytes 12582920 | tf_op jit(solution)/shard_map/ppermute | solution.py:14
  203.1 180.2 %collective-permute-done.3 = bf16[32,4,128,128]{3,2,1,0:T(8,128)(2,1)} collective-permute-done((bf16[32,4,128,128]{3,2,1,0:T(8,128)(2,1)}, bf16[32,4,128,128]{3,2,1,0:T(8,128)(2,1)}, u32[]{:S(2)}, u32[]{:S(2)}) %collective-permute-start.3) | collective-permute-done | bytes 4194336 | tf_op jit(solution)/shard_map/ppermute | solution.py:14
  383.3 2.6 broadcast_select_fusion.1
  385.9 2.0 copy-done.4
  387.9 1.2 collective-permute-start.5
  389.1 92.5 %collective-permute-done.5 = bf16[32,4,128,128]{3,2,1,0:T(8,128)(2,1)} collective-permute-done((bf16[32,4,128,128]{3,2,1,0:T(8,128)(2,1)S(1)}, bf16[32,4,128,128]{3,2,1,0:T(8,128)(2,1)}, u32[]{:S(2)}, u32[]{:S(2)}) %collective-permute-start.5) | collective-permute-done | bytes 4194336 | tf_op jit(solution)/shard_map/ppermute | solution.py:14
  482.0 0.7 gather_fusion
  483.0 0.7 scatter_custom_fusion
  483.7 1.2 gather_fusion.1
  485.1 2.1 collective-permute-start
  487.2 1.9 slice.7
  489.2 0.6 gather_fusion.3
  490.0 92.1 %collective-permute-done.7 = bf16[32,4,128,128]{3,2,1,0:T(8,128)(2,1)} collective-permute-done((bf16[32,4,128,128]{3,2,1,0:T(8,128)(2,1)}, bf16[32,4,128,128]{3,2,1,0:T(8,128)(2,1)}, u32[]{:S(2)}, u32[]{:S(2)}) %collective-permute-start.7) | collective-permute-done | bytes 4194336 | tf_op jit(solution)/shard_map/ppermute | solution.py:14
  582.1 2.2 collective-permute-start.9
  584.3 0.7 gather_fusion.4
  585.2 94.4 %all-gather.1 = s32[4,4,4]{2,1,0:T(4,128)S(1)} all-gather(s32[1,4,4]{2,1,0:T(4,128)S(1)} %bitcast.168), channel_id=1, replica_groups=mesh['row'=16,'col'=4,'layer'=4] {'col'}, dimensions={0}, use_global_device_ids=true | all-gather | bytes 320 | tf_op jit(solution)/shard_map/all_gather | solution.py:84
  680.4 5.3 collective-permute-start.1
  685.7 1.4 collective-permute-done.1
  687.1 4.7 collective-permute-done.4
  691.8 4.7 collective-permute-done.6
  696.5 0.6 gather_fusion.2
  697.1 0.6 gather_fusion.6
  697.6 0.6 gather_fusion.8
  698.2 3.0 collective-permute-done.8
  701.2 0.6 gather_fusion.10
  701.8 2.8 gather_fusion.5
  704.6 0.6 convolution_convert_fusion.7
  705.3 1.4 fusion.20
  706.7 2.8 gather_fusion.7
  709.6 0.6 convolution_convert_fusion.6
  710.2 2.8 fusion.18
  713.0 2.8 gather_fusion.9
  715.8 0.6 convolution_convert_fusion.5
  716.5 2.8 fusion.16
  719.2 2.8 gather_fusion.11
  722.1 0.6 convolution_convert_fusion.4
  722.7 4.2 add_bitcast_fusion
  727.0 2.9 copy.32
  730.0 88.5 %all-gather.11.cloned.1.call-done = f32[16,8,128,128]{3,2,1,0:T(8,128)} async-done(((f32[4,8,128,128]{3,2,1,0:T(8,128)}), f32[16,8,128,128]{3,2,1,0:T(8,128)}) %all-gather.11.cloned.1.call-update) | async-done | bytes 8388624 | tf_op jit(solution)/shard_map/all_gather | solution.py:100
  818.5 4.4 reduce_sum.9
  822.9 1.2 convert_element_type.44
  824.3 7.6 all-gather.2
  832.4 0.6 gather_fusion.12
  833.0 0.6 gather_fusion.14
  834.1 0.6 gather_fusion.18
  834.7 3.0 gather_fusion.13
  837.6 2.2 convolution_convert_fusion.3
  839.9 3.1 gather_fusion.15
  843.0 2.2 convolution_convert_fusion.2
  845.2 3.0 gather_fusion.17
  848.2 2.2 convolution_convert_fusion.1
  850.5 3.0 gather_fusion.19
  853.4 2.2 convolution_convert_fusion
  855.6 11.3 %all-gather.9.cloned.1.call-done = bf16[4,32,128,128]{3,2,1,0:T(8,128)(2,1)} async-done(((bf16[4,8,128,128]{3,2,1,0:T(8,128)(2,1)}), bf16[4,32,128,128]{3,2,1,0:T(8,128)(2,1)}) %all-gather.9.cloned.1.call-update) | async-done | bytes 4194320 | tf_op jit(solution)/shard_map/all_gather | solution.py:83
  866.9 2.7 fusion.3
  869.6 2.0 fusion.5
  871.7 2.0 fusion.1
  873.7 3.3 fusion
  877.3 31.2 %reduce-scatter.2.cloned.1.call-done = f32[1,8,128,128]{2,3,1,0:T(8,128)} async-done(((f32[4,8,128,128]{2,3,1,0:T(8,128)}), f32[1,8,128,128]{2,3,1,0:T(8,128)}) %reduce-scatter.2.cloned.1.call-update) | async-done | bytes 524304 | tf_op jit(solution)/shard_map/reduce_scatter | solution.py:104
  908.5 1.1 multiply_subtract_fusion
  909.6 1.0 copy.44
  (81 shorter events, 3.4 us)
Async XLA Ops:
  6.5 698.7 %all-gather.7.cloned.1.call-start = ((), (), s32[]{:S(2)}) async-start(), calls=%async_computation.1 | async-start | bytes 2621440 | tf_op jit(solution)/shard_map/all_gather | solution.py:83
  6.5 133.8 %collective-permute-start.2 = (bf16[32,4,128,128]{3,2,1,0:T(8,128)(2,1)}, bf16[32,4,128,128]{3,2,1,0:T(8,128)(2,1)}, u32[]{:S(2)}, u32[]{:S(2)}) collective-permute-start(bf16[32,4,128,128]{3,2,1,0:T(8,128)(2,1)} %param.4), channel_id=1, source_target_pairs={{0,64},{16,80},{32,96},{48,112},{64,128},{80,144},{96,160},{112,17... | collective-permute-start | bytes 12582920 | tf_op jit(solution)/shard_map/ppermute | solution.py:14
  144.9 238.4 %collective-permute-start.3 = (bf16[32,4,128,128]{3,2,1,0:T(8,128)(2,1)}, bf16[32,4,128,128]{3,2,1,0:T(8,128)(2,1)}, u32[]{:S(2)}, u32[]{:S(2)}) collective-permute-start(bf16[32,4,128,128]{3,2,1,0:T(8,128)(2,1)} %broadcast_select_fusion), channel_id=1, source_target_pairs={{0,128},{16,144},{32,160},{48,176},{64,192},{80,208},{96,224},{112... | collective-permute-start | bytes 12582920 | tf_op jit(solution)/shard_map/ppermute | solution.py:14
  203.1 279.0 %copy-start = (s32[32]{0:T(128)S(1)}, s32[32]{0:T(128)}, u32[]{:S(2)}) copy-start(s32[32]{0:T(128)} %param.7) | copy-start | bytes 388
  203.1 279.7 %copy-start.5 = (s32[32,4]{0,1:T(4,128)S(1)}, s32[32,4]{0,1:T(4,128)}, u32[]{:S(2)}) copy-start(s32[32,4]{0,1:T(4,128)} %param.5) | copy-start | bytes 1540
  385.9 2.0 copy-start.4
  387.9 93.8 %collective-permute-start.5 = (bf16[32,4,128,128]{3,2,1,0:T(8,128)(2,1)S(1)}, bf16[32,4,128,128]{3,2,1,0:T(8,128)(2,1)}, u32[]{:S(2)}, u32[]{:S(2)}) collective-permute-start(bf16[32,4,128,128]{3,2,1,0:T(8,128)(2,1)S(1)} %broadcast_select_fusion.1), channel_id=1, source_target_pairs={{0,16},{16,32},{32,48},{48,64},{64,80},{80,96},{96,112},{112,128},... | collective-permute-start | bytes 12582920 | tf_op jit(solution)/shard_map/ppermute | solution.py:14
  481.6 100.5 %collective-permute-start.7 = (bf16[32,4,128,128]{3,2,1,0:T(8,128)(2,1)}, bf16[32,4,128,128]{3,2,1,0:T(8,128)(2,1)}, u32[]{:S(2)}, u32[]{:S(2)}) collective-permute-start(bf16[32,4,128,128]{3,2,1,0:T(8,128)(2,1)} %collective-permute-done.5), channel_id=1, source_target_pairs={{0,16},{16,32},{32,48},{48,64},{64,80},{80,96},{96,112},{112,128},... | collective-permute-start | bytes 12582920 | tf_op jit(solution)/shard_map/ppermute | solution.py:14
  484.9 4.9 copy-start.6
  485.1 195.3 %collective-permute-start = (s32[32,4]{1,0:T(8,128)S(1)}, s32[32,4]{1,0:T(8,128)S(1)}, u32[]{:S(2)}, u32[]{:S(2)}) collective-permute-start(s32[32,4]{1,0:T(8,128)S(1)} %broadcast_add_fusion), channel_id=1, source_target_pairs={{0,64},{16,80},{32,96},{48,112},{64,128},{80,144},{96,160},{112,17... | collective-permute-start | bytes 1544 | tf_op jit(solution)/shard_map/ppermute | solution.py:14
  489.1 329.4 %all-gather.11.cloned.1.call-start = ((), (), s32[]{:S(2)}) async-start(), calls=%async_computation.4 | async-start | bytes 10485760 | tf_op jit(solution)/shard_map/all_gather | solution.py:100
  582.1 137.1 %collective-permute-start.9 = (bf16[32,4,128,128]{3,2,1,0:T(8,128)(2,1)}, bf16[32,4,128,128]{3,2,1,0:T(8,128)(2,1)}, u32[]{:S(2)}, u32[]{:S(2)}) collective-permute-start(bf16[32,4,128,128]{3,2,1,0:T(8,128)(2,1)} %collective-permute-done.7), channel_id=1, source_target_pairs={{0,16},{16,32},{32,48},{48,64},{64,80},{80,96},{96,112},{112,128},... | collective-permute-start | bytes 12582920 | tf_op jit(solution)/shard_map/ppermute | solution.py:14
  680.4 6.7 collective-permute-start.1
  687.1 4.7 collective-permute-start.4
  691.8 4.7 collective-permute-start.6
  696.5 4.7 collective-permute-start.8
  729.9 137.0 %all-gather.9.cloned.1.call-start = ((), (), s32[]{:S(2)}) async-start(), calls=%async_computation.2 | async-start | bytes 5242880 | tf_op jit(solution)/shard_map/all_gather | solution.py:83
  824.2 84.3 %reduce-scatter.2.cloned.1.call-start = ((), (), s32[]{:S(2)}) async-start(), calls=%async_computation.3 | async-start | bytes 2621440 | tf_op jit(solution)/shard_map/reduce_scatter | solution.py:104
  866.9 2.7 copy-start.1
  869.6 2.0 copy-start.2
  871.6 2.0 copy-start.3
Sparse Core Ops, SparseCore 0:
  489.2 41.7 all-gather.6
  730.0 88.4 all-gather.10
  824.3 42.5 all-gather.8
  877.1 31.2 reduce-scatter.1
